TPU v7x, 512 devices: a whole 4x8x8 slice. The times are simulated.
512 devices in a mesh: segment: 4 (over z_lo), seq: 16 (over z_hi, x, core), mp: 8 (over y).
Axes of the slice: x: 4, y: 8, z: 8 (z_hi: 2, z_lo: 4; z = z_hi * 4 + z_lo), core: 2. Of those that a mesh axis runs over, the one named last changes fastest.
Arguments:
- latents: bfloat16 [4, 16, 256, 4096], P('segment', 'seq', None, 'mp'), may hold values from -6 to 6
- w_qkv: bfloat16 [4, 4096, 3, 4096], P('segment', 'seq', None, 'mp'), may hold values from -1 to 1
- w_out: bfloat16 [4, 4096, 4096], P('segment', 'mp', 'seq'), may hold values from -0.09375 to 0.09375
- mod_shift: float32 [4, 4096], P('segment'), may hold values from -3 to 3
- mod_scale: float32 [4, 4096], P('segment'), may hold values from 0.1 to 1.9
- mod_gate: float32 [4, 4096], P('segment'), may hold values from 0.5 to 1.5
- counts: int32 [4, 16], P('segment'), may hold values from 64 to 256, as said below
Outputs:
- next_latents: bfloat16 [4, 16, 256, 4096], P('segment', 'seq', None, 'mp')
Inputs may be any that keep to these rules, and one draw needn't show every extreme that they name: `counts`: in every section's clip at least one frame has all 256 patch positions valid.
All inputs are finite; a program needn't handle non-finite values.
Results may differ from a plain program's by a relative error of at most 0.01.
Values may be sent and summed in bfloat16 or wider, within the bound.
No kernel may reach another device: no remote copies, remote signals or barrier semaphores. Data moves between devices by JAX's collectives and lax.ppermute only.
A program may use at most 64 MiB of HBM per device.

v0:
```python
import math
import jax
import jax.numpy as jnp
from jax import lax
from jax.sharding import PartitionSpec as P

HD = 128
EPS = 1e-06
NEG_FILL = -1e30


def passed_along(x, axis, by):
    length = lax.axis_size(axis)
    return lax.ppermute(x, axis, [(i, (i + by) % length) for i in range(length)])


def masked_attention(queries, keys_in, values, usable):
    factor = 1.0 / math.sqrt(queries.shape[-1])
    scores = (
        jnp.einsum("...ihe,...jhe->...hij", queries, keys_in, preferred_element_type=jnp.float32)
        * factor
    )
    allowed = usable[..., None, :, None] & usable[..., None, None, :]
    masked = jnp.where(allowed, scores, NEG_FILL)
    highest = jnp.max(masked, axis=-1, keepdims=True)
    raised = jnp.where(allowed, jnp.exp(masked - highest), 0.0)
    spare_one = jnp.where(usable, 0.0, 1.0)[..., None, :, None]
    weights = (raised / (jnp.sum(raised, axis=-1, keepdims=True) + spare_one)).astype(jnp.bfloat16)
    blended = jnp.einsum(
        "...hij,...jhe->...ihe", weights, values, preferred_element_type=jnp.float32
    )
    return blended.astype(jnp.bfloat16)


def relay_features(rows_now):
    return lax.all_to_all(rows_now, "seq", split_axis=0, concat_axis=0, tiled=True)


def pass_onward(rows_now):
    return passed_along(rows_now, "segment", 1)


def on_device(latents, w_qkv, w_out, mod_shift, mod_scale, mod_gate, counts):
    frames = lax.axis_size("seq")
    patches = latents.shape[2]
    narrow = latents.shape[3]
    span = patches // frames
    segment_rows = latents[0, 0]
    gathered = lax.all_gather(latents, "mp", axis=3, tiled=True)[0, 0]
    widened = gathered.astype(jnp.float32)
    average = jnp.mean(widened, axis=-1, keepdims=True)
    centred = widened - average
    variance = jnp.mean(centred * centred, axis=-1, keepdims=True)
    modulated = (centred * lax.rsqrt(variance + EPS) * mod_scale[0] + mod_shift[0]).astype(
        jnp.bfloat16
    )
    columns = w_qkv.shape[2] * w_qkv.shape[3]
    piece = lax.all_gather(w_qkv, "seq", axis=1, tiled=True)
    height = piece.shape[1]
    projected = jnp.dot(
        modulated, piece.reshape(height, columns), preferred_element_type=jnp.float32
    )
    local_heads = w_qkv.shape[3] // HD
    projected = projected.astype(jnp.bfloat16).reshape(patches, 3, local_heads, HD)
    frame_here = lax.axis_index("seq")
    clip_counts = counts[0]
    positions = jnp.arange(frames)

    def spatial(triple):
        count_here = jnp.sum(jnp.where(positions == frame_here, clip_counts, 0))
        usable = jnp.arange(patches) < count_here
        return masked_attention(triple[:, 0], triple[:, 1], triple[:, 2], usable)

    def temporal(triple):
        by_place = triple.reshape(frames, span, 3, local_heads, HD).transpose(1, 0, 2, 3, 4)
        location = frame_here * span + jnp.arange(span)
        usable = location[:, None] < clip_counts[None, :]
        blended = masked_attention(by_place[:, :, 0], by_place[:, :, 1], by_place[:, :, 2], usable)
        return blended.transpose(1, 0, 2, 3).reshape(patches, local_heads, HD)

    attended = lax.cond(lax.axis_index("segment") % 2 == 0, spatial, temporal, projected)
    attended = attended.reshape(patches, local_heads * HD)
    out_whole = lax.all_gather(w_out, "seq", axis=2, tiled=True)[0]
    member = lax.axis_index("mp")
    partials = jnp.dot(attended, out_whole, preferred_element_type=jnp.float32)
    summed = lax.psum_scatter(
        partials.astype(jnp.bfloat16), "mp", scatter_dimension=1, tiled=True
    ).astype(jnp.float32)
    gate_here = lax.dynamic_slice_in_dim(mod_gate[0], member * narrow, narrow)
    updated = (segment_rows.astype(jnp.float32) + gate_here * summed).astype(jnp.bfloat16)
    updated = updated.reshape(frames, span, narrow)
    moved = pass_onward(relay_features(updated))
    return moved.reshape(1, 1, patches, narrow)


def solution(mesh):
    return jax.shard_map(
        on_device,
        mesh=mesh,
        in_specs=(
            P("segment", "seq", None, "mp"),
            P("segment", "seq", None, "mp"),
            P("segment", "mp", "seq"),
            P("segment", None),
            P("segment", None),
            P("segment", None),
            P("segment", None),
        ),
        out_specs=P("segment", "seq", None, "mp"),
        check_vma=False,
    )
```

profile of v0, /device:TPU:1, one launch (start us, length us, event | category | flops | bytes accessed | tf_op | source)
XLA Modules:
  0.0 384.6 jit_solution(8186895898152812026)
XLA Ops:
  6.5 0.7 all-gather.4.cloned.1.call-update
  7.3 2.3 copy.18
  9.7 0.7 all-gather.8.cloned.1.call-update
  10.5 43.7 %all-gather.4.cloned.1.call-done = bf16[1,1,256,4096]{3,2,1,0:T(8,128)(2,1)} async-done(((bf16[1,1,256,512]{3,2,1,0:T(8,128)(2,1)}), bf16[1,1,256,4096]{3,2,1,0:T(8,128)(2,1)}) %all-gather.4.cloned.1.call-update) | async-done | bytes 2097168 | tf_op jit(solution)/shard_map/all_gather | solution.py:49
  54.1 2.1 convert_reduce_fusion
  56.2 2.3 fusion.30
  58.5 157.1 %all-gather.6.cloned.1.call-done = bf16[1,4096,3,512]{1,3,2,0:T(8,128)(2,1)} async-done(((bf16[1,256,3,512]{1,3,2,0:T(8,128)(2,1)}), bf16[1,4096,3,512]{1,3,2,0:T(8,128)(2,1)}) %all-gather.6.cloned.1.call-update) | async-done | bytes 12582928 | tf_op jit(solution)/shard_map/all_gather | solution.py:58
  215.7 8.2 %convolution_convert_fusion.3 = bf16[256,1536]{1,0:T(8,128)(2,1)S(1)} fusion(bf16[4096,1536]{0,1:T(8,128)(2,1)} %bitcast.96, bf16[1,1,256,4096]{3,2,1,0:T(8,128)(2,1)S(1)} %copy-done.1, f32[4096]{0:T(1024)S(1)} %bitcast.97, f32[4096]{0:T(1024)S(1)} %bitcast.98, f32[256]{0:T(256)S(1)} %add_rsqrt_fusion, f32[256]{0:T(256)S(1)} %broadcast_multiply_fusion), kind=kOutput, calls=%fused_computation.58 | convolution fusion | flops 3227910144 | bytes 15501312 | tf_op jit(solution)/shard_map/dot_general | solution.py:60
  223.9 3.7 conditional.1
  223.9 0.6 fusion.14
  224.6 0.6 iota_compare_fusion
  225.1 0.1 broadcast_and_fusion.1
  225.2 0.3 copy.19
  225.5 0.6 fusion.40
  226.2 0.6 broadcast_select_fusion.1
  226.7 0.8 convolution_convert_fusion.1
  227.6 71.0 %all-gather.8.cloned.1.call-done = bf16[1,512,4096]{2,1,0:T(8,128)(2,1)} async-done(((bf16[1,512,256]{2,1,0:T(8,128)(2,1)}), bf16[1,512,4096]{2,1,0:T(8,128)(2,1)}) %all-gather.8.cloned.1.call-update) | async-done | bytes 4194320 | tf_op jit(solution)/shard_map/all_gather | solution.py:83
  298.5 4.8 %convolution_convert_fusion.2 = bf16[256,4096]{1,0:T(8,128)(2,1)} fusion(bf16[256,512]{0,1:T(8,128)(2,1)S(1)} %get-tuple-element.36, bf16[1,512,4096]{2,1,0:T(8,128)(2,1)} %all-gather.8.cloned.1.call-done), kind=kOutput, calls=%fused_computation.49 | convolution fusion | flops 1074790400 | bytes 6553600 | tf_op jit(solution)/shard_map/dot_general | solution.py:85
  303.4 36.3 %reduce-scatter.2.cloned.1.call-done = bf16[256,512]{1,0:T(8,128)(2,1)} async-done(((bf16[256,4096]{1,0:T(8,128)(2,1)}), bf16[256,512]{1,0:T(8,128)(2,1)}) %reduce-scatter.2.cloned.1.call-update) | async-done | bytes 262160 | tf_op jit(solution)/shard_map/reduce_scatter | solution.py:86
  339.7 1.0 fusion.38
  340.7 26.0 %all_to_all.5 = bf16[16,16,512]{2,1,0:T(8,128)(2,1)S(1)} all-to-all(bf16[16,16,512]{2,1,0:T(8,128)(2,1)S(1)} %bitcast.84), channel_id=1, replica_groups=mesh['segment'=4,'seq'=16,'mp'=8] {'seq'}, dimensions={0} | all-to-all | bytes 524288 | tf_op jit(solution)/shard_map/all_to_all | solution.py:36
  366.8 5.0 %collective-permute-start = (bf16[16,16,512]{2,1,0:T(8,128)(2,1)S(1)}, bf16[16,16,512]{2,1,0:T(8,128)(2,1)S(1)}, u32[]{:S(2)}, u32[]{:S(2)}) collective-permute-start(bf16[16,16,512]{2,1,0:T(8,128)(2,1)S(1)} %all_to_all.5), channel_id=1, source_target_pairs={{0,128},{128,256},{256,384},{384,0},{1,129},{129,257},{257,385},{3... | collective-permute-start | bytes 786440 | tf_op jit(solution)/shard_map/ppermute | solution.py:14
  371.7 5.6 %collective-permute-done = bf16[16,16,512]{2,1,0:T(8,128)(2,1)S(1)} collective-permute-done((bf16[16,16,512]{2,1,0:T(8,128)(2,1)S(1)}, bf16[16,16,512]{2,1,0:T(8,128)(2,1)S(1)}, u32[]{:S(2)}, u32[]{:S(2)}) %collective-permute-start) | collective-permute-done | bytes 262176 | tf_op jit(solution)/shard_map/ppermute | solution.py:14
  377.4 0.7 copy.32
  (23 shorter events, 0.2 us)
Async XLA Ops:
  6.5 296.9 %copy-start = (f32[1,4096]{1,0:T(1,128)S(1)}, f32[1,4096]{1,0:T(1,128)}, u32[]{:S(2)}) copy-start(f32[1,4096]{1,0:T(1,128)} %param.14) | copy-start | bytes 49156
  6.5 209.1 %copy-start.5 = (f32[1,4096]{1,0:T(1,128)S(1)}, f32[1,4096]{1,0:T(1,128)}, u32[]{:S(2)}) copy-start(f32[1,4096]{1,0:T(1,128)} %param.13) | copy-start | bytes 49156
  6.5 209.1 %copy-start.4 = (f32[1,4096]{1,0:T(1,128)S(1)}, f32[1,4096]{1,0:T(1,128)}, u32[]{:S(2)}) copy-start(f32[1,4096]{1,0:T(1,128)} %param.12) | copy-start | bytes 49156
  6.5 47.6 %all-gather.4.cloned.1.call-start = ((), (), s32[]{:S(2)}) async-start(), calls=%async_computation.2 | async-start | bytes 2359296 | tf_op jit(solution)/shard_map/all_gather | solution.py:49
  7.3 208.4 %all-gather.6.cloned.1.call-start = ((), (), s32[]{:S(2)}) async-start(), calls=%async_computation.3 | async-start | bytes 13369344 | tf_op jit(solution)/shard_map/all_gather | solution.py:58
  9.7 288.9 %all-gather.8.cloned.1.call-start = ((), (), s32[]{:S(2)}) async-start(), calls=%async_computation.4 | async-start | bytes 4456448 | tf_op jit(solution)/shard_map/all_gather | solution.py:83
  10.4 329.3 %reduce-scatter.2.cloned.1.call-start = ((), (), s32[]{:S(2)}) async-start(), calls=%async_computation.5 | async-start | bytes 2359296 | tf_op jit(solution)/shard_map/reduce_scatter | solution.py:86
  54.1 161.5 %copy-start.1 = (bf16[1,1,256,4096]{3,2,1,0:T(8,128)(2,1)S(1)}, bf16[1,1,256,4096]{3,2,1,0:T(8,128)(2,1)}, u32[]{:S(2)}) copy-start(bf16[1,1,256,4096]{3,2,1,0:T(8,128)(2,1)} %all-gather.4.cloned.1.call-done) | copy-start | bytes 6291460
  215.7 8.3 %copy-start.3 = (s32[1,16]{1,0:T(1,128)S(1)}, s32[1,16]{1,0:T(1,128)}, u32[]{:S(2)}) copy-start(s32[1,16]{1,0:T(1,128)} %param.15) | copy-start | bytes 196
  227.6 112.1 %copy-start.2 = (bf16[1,1,256,512]{3,2,1,0:T(8,128)(2,1)S(1)}, bf16[1,1,256,512]{3,2,1,0:T(8,128)(2,1)}, u32[]{:S(2)}) copy-start(bf16[1,1,256,512]{3,2,1,0:T(8,128)(2,1)} %param.9) | copy-start | bytes 786436
  366.8 10.6 %collective-permute-start = (bf16[16,16,512]{2,1,0:T(8,128)(2,1)S(1)}, bf16[16,16,512]{2,1,0:T(8,128)(2,1)S(1)}, u32[]{:S(2)}, u32[]{:S(2)}) collective-permute-start(bf16[16,16,512]{2,1,0:T(8,128)(2,1)S(1)} %all_to_all.5), channel_id=1, source_target_pairs={{0,128},{128,256},{256,384},{384,0},{1,129},{129,257},{257,385},{3... | collective-permute-start | bytes 786440 | tf_op jit(solution)/shard_map/ppermute | solution.py:14
Sparse Core Ops, SparseCore 0:
  9.4 44.6 all-gather.3
  57.3 158.3 all-gather.5
  218.8 79.7 all-gather.7
  303.5 36.1 reduce-scatter.1
where the time goes:
time: 385 us
  waiting for transfers between devices  315 us (82%)
  blocking collectives  26 us (7%)
  matrix products  14.5 us (4%)
  between operations  13.2 us (3%)
  other arithmetic  7.29 us (2%)
  starting transfers between devices  5.07 us (1%)
    all_gather x1, waiting for transfers between devices, on_device(): piece = lax.all_gather(w_qkv, 'seq', axis=1, tiled=True)  157 us
    all_gather x1, waiting for transfers between devices, on_device(): out_whole = lax.all_gather(w_out, 'seq', axis=2, tiled=True)[0]  71 us
    all_gather x1, waiting for transfers between devices, on_device(): gathered = lax.all_gather(latents, 'mp', axis=3, tiled=True)[0, 0]  43.7 us
    reduce_scatter x1, waiting for transfers between devices, on_device(): lax.psum_scatter(partials.astype(jnp.bfloat16), 'mp', scatter_dimension=1...  36.3 us
    all_to_all x1, blocking collectives, relay_features(): lax.all_to_all(rows_now, 'seq', split_axis=0, concat_axis=0, tiled=True)  26 us
    dot_general x1, matrix products, on_device(): jnp.dot(modulated, piece.reshape(height, columns), preferred_element_type...  8.22 us
  transfers between devices with their start and end apart: 5, of which 5 were waited for; matrix products, arithmetic and copies ran while one was open for 5% of the time, Pallas kernels for 0%

commit v1 on v0

--- a/solution.py
+++ b/solution.py
@@ -46,7 +46,33 @@
     narrow = latents.shape[3]
     span = patches // frames
     segment_rows = latents[0, 0]
-    gathered = lax.all_gather(latents, "mp", axis=3, tiled=True)[0, 0]
+
+    def _time_screen(mine):
+        carry, u_next, seen_now = (lax.axis_size("mp"), lax.axis_index("mp"), mine.shape[3])
+        inbox = tuple((j * carry if idx == 3 else j for idx, j in enumerate(mine.shape)))
+        local_next = lax.dynamic_update_slice_in_dim(
+            jnp.zeros(inbox, mine.dtype), mine, u_next * seen_now, axis=3
+        )
+        mid_arr = block_next = mine
+        dev_j = 1
+        while dev_j < carry // 2 + 1:
+            mid_arr = lax.ppermute(
+                mid_arr, "mp", tuple(((idx, (idx + 1) % carry) for idx in range(carry)))
+            )
+            local_next = lax.dynamic_update_slice_in_dim(
+                local_next, mid_arr, (u_next - dev_j) % carry * seen_now, axis=3
+            )
+            if 2 * dev_j < carry:
+                block_next = lax.ppermute(
+                    block_next, "mp", tuple(((idx, (idx - 1) % carry) for idx in range(carry)))
+                )
+                local_next = lax.dynamic_update_slice_in_dim(
+                    local_next, block_next, (u_next + dev_j) % carry * seen_now, axis=3
+                )
+            dev_j += 1
+        return local_next
+
+    gathered = _time_screen(latents)[0, 0]
     widened = gathered.astype(jnp.float32)
     average = jnp.mean(widened, axis=-1, keepdims=True)
     centred = widened - average

time: 385 us -> 341 us (0.89)
  waiting for transfers between devices: 315 us -> 250 us
  starting transfers between devices: 5.07 us -> 28.3 us
    all_gather x1 -> x0, waiting for transfers between devices: 43.7 us -> none  [on_device(): gathered = lax.all_gather(latents, 'mp', axis=3, tiled=True)[0, 0]]
    all_gather x1, waiting for transfers between devices: 157 us -> 122 us  [on_device(): piece = lax.all_gather(w_qkv, 'seq', axis=1, tiled=True)]
    ppermute x0 -> x7, starting transfers between devices: none -> 23.5 us  [the longest x3 13.1 us: _time_screen(): lax.ppermute(block_next, 'mp', tuple(((idx, (idx - 1) % carry) for idx in...]
    ppermute x0 -> x7, waiting for transfers between devices: none -> 14.4 us  [the longest x4 14.4 us: _time_screen(): lax.ppermute(mid_arr, 'mp', tuple(((idx, (idx + 1) % carry) for idx in ra...]
  transfers between devices with their start and end apart: 5 -> 11, of which waited for: 5 -> 8; matrix products, arithmetic and copies ran while one was open for 5% -> 4% of each run, Pallas kernels for 0% -> 0%
where the time goes in v1:
time: 341 us; the launch traced here: 340 us
  waiting for transfers between devices  250 us (73%)
  starting transfers between devices  28.3 us (8%)
  blocking collectives  26 us (8%)
  matrix products  14.3 us (4%)
  between operations  13.5 us (4%)
  other arithmetic  3.97 us (1%)
  local copies, waits for them, and re-layouts  3.79 us (1%)
    all_gather x1, waiting for transfers between devices, on_device(): piece = lax.all_gather(w_qkv, 'seq', axis=1, tiled=True)  122 us
    all_gather x1, waiting for transfers between devices, on_device(): out_whole = lax.all_gather(w_out, 'seq', axis=2, tiled=True)[0]  71.1 us
    reduce_scatter x1, waiting for transfers between devices, on_device(): lax.psum_scatter(partials.astype(jnp.bfloat16), 'mp', scatter_dimension=1...  36.3 us
    all_to_all x1, blocking collectives, relay_features(): lax.all_to_all(rows_now, 'seq', split_axis=0, concat_axis=0, tiled=True)  26 us
    ppermute x4, waiting for transfers between devices, _time_screen(): lax.ppermute(mid_arr, 'mp', tuple(((idx, (idx + 1) % carry) for idx in ra...  14.4 us
    ppermute x3, starting transfers between devices, _time_screen(): lax.ppermute(block_next, 'mp', tuple(((idx, (idx - 1) % carry) for idx in...  13.1 us
    ppermute x4, starting transfers between devices, _time_screen(): lax.ppermute(mid_arr, 'mp', tuple(((idx, (idx + 1) % carry) for idx in ra...  10.4 us
    dot_general x1, matrix products, on_device(): jnp.dot(modulated, piece.reshape(height, columns), preferred_element_type...  8.06 us
  transfers between devices with their start and end apart: 11, of which 8 were waited for; matrix products, arithmetic and copies ran while one was open for 4% of the time, Pallas kernels for 0%

profile of v1, /device:TPU:1, one launch (start us, length us, event | category | flops | bytes accessed | tf_op | source)
XLA Modules:
  0.0 340.3 jit_solution(15700937758997261299)
XLA Ops:
  6.5 2.3 copy.18
  9.7 4.0 %collective-permute-start = (bf16[1,1,256,512]{3,2,1,0:T(8,128)(2,1)S(1)}, bf16[1,1,256,512]{3,2,1,0:T(8,128)(2,1)S(1)}, u32[]{:S(2)}, u32[]{:S(2)}) collective-permute-start(bf16[1,1,256,512]{3,2,1,0:T(8,128)(2,1)S(1)} %copy-done.1), channel_id=1, source_target_pairs={{0,1},{1,2},{2,3},{3,4},{4,5},{5,6},{6,7},{7,0},{8,9},{9,10},{10,1... | collective-permute-start | bytes 786440 | tf_op jit(solution)/shard_map/ppermute | solution.py:59
  13.7 3.8 %collective-permute-start.1 = (bf16[1,1,256,512]{3,2,1,0:T(8,128)(2,1)S(1)}, bf16[1,1,256,512]{3,2,1,0:T(8,128)(2,1)S(1)}, u32[]{:S(2)}, u32[]{:S(2)}) collective-permute-start(bf16[1,1,256,512]{3,2,1,0:T(8,128)(2,1)S(1)} %copy-done.1), channel_id=1, source_target_pairs={{0,7},{1,0},{2,1},{3,2},{4,3},{5,4},{6,5},{7,6},{8,15},{9,8},{10,9... | collective-permute-start | bytes 786440 | tf_op jit(solution)/shard_map/ppermute | solution.py:66
  18.0 1.4 collective-permute-done
  19.4 2.5 collective-permute-start.2
  21.9 4.7 %collective-permute-start.3 = (bf16[1,1,256,512]{3,2,1,0:T(8,128)(2,1)S(1)}, bf16[1,1,256,512]{3,2,1,0:T(8,128)(2,1)S(1)}, u32[]{:S(2)}, u32[]{:S(2)}) collective-permute-start(bf16[1,1,256,512]{3,2,1,0:T(8,128)(2,1)S(1)} %collective-permute-done.1), channel_id=1, source_target_pairs={{0,7},{1,0},{2,1},{3,2},{4,3},{5,4},{6,5},{7,6},{8,15},{9,8},{10,9... | collective-permute-start | bytes 786440 | tf_op jit(solution)/shard_map/ppermute | solution.py:66
  26.7 1.7 collective-permute-done.2
  28.4 1.9 collective-permute-start.4
  30.4 4.6 %collective-permute-start.5 = (bf16[1,1,256,512]{3,2,1,0:T(8,128)(2,1)S(1)}, bf16[1,1,256,512]{3,2,1,0:T(8,128)(2,1)S(1)}, u32[]{:S(2)}, u32[]{:S(2)}) collective-permute-start(bf16[1,1,256,512]{3,2,1,0:T(8,128)(2,1)S(1)} %collective-permute-done.3), channel_id=1, source_target_pairs={{0,7},{1,0},{2,1},{3,2},{4,3},{5,4},{6,5},{7,6},{8,15},{9,8},{10,9... | collective-permute-start | bytes 786440 | tf_op jit(solution)/shard_map/ppermute | solution.py:66
  35.0 3.0 collective-permute-done.4
  38.0 1.9 collective-permute-start.6
  40.0 8.3 %collective-permute-done.6 = bf16[1,1,256,512]{3,2,1,0:T(8,128)(2,1)S(1)} collective-permute-done((bf16[1,1,256,512]{3,2,1,0:T(8,128)(2,1)S(1)}, bf16[1,1,256,512]{3,2,1,0:T(8,128)(2,1)S(1)}, u32[]{:S(2)}, u32[]{:S(2)}) %collective-permute-start.6) | collective-permute-done | bytes 262176 | tf_op jit(solution)/shard_map/ppermute | solution.py:59
  49.4 122.0 %all-gather.3.cloned.1.call-done = bf16[1,4096,3,512]{1,3,2,0:T(8,128)(2,1)} async-done(((bf16[1,256,3,512]{1,3,2,0:T(8,128)(2,1)}), bf16[1,4096,3,512]{1,3,2,0:T(8,128)(2,1)}) %all-gather.3.cloned.1.call-update) | async-done | bytes 12582928 | tf_op jit(solution)/shard_map/all_gather | solution.py:84
  171.4 8.1 %convolution_convert_fusion.3 = bf16[256,1536]{1,0:T(8,128)(2,1)S(1)} fusion(bf16[4096,1536]{0,1:T(8,128)(2,1)} %bitcast.99, bf16[256,4096]{1,0:T(8,128)(2,1)S(1)} %bitcast_dynamic-update-slice_fusion, f32[4096]{0:T(1024)S(1)} %bitcast.100, f32[4096]{0:T(1024)S(1)} %bitcast.101, f32[256]{0:T(256)S(1)} %add_rsqrt_fusion, f32[256]{0:T(256)S(1)} %broadcast_multiply_fusion), kind=kOutput, calls=%fused_computation.56 | convolution fusion | flops 3227910144 | bytes 15501312 | tf_op jit(solution)/shard_map/dot_general | solution.py:86
  179.5 3.7 %conditional.1 = (bf16[256,512]{0,1:T(8,128)(2,1)S(1)}) conditional(s32[]{:T(128)} %convert_element_type.44, (s32[]{:T(128)}, s32[1,16]{1,0:T(1,128)S(1)}, bf16[256,1536]{1,0:T(8,128)(2,1)S(1)}) %tuple.24, (s32[]{:T(128)}, s32[16]{0:T(128)S(1)}, s32[1,16]{1,0:T(1,128)S(1)}, bf16[256,1536]{1,0:T(8,128)(2,1)S(1)}) %tuple.25), branch_computations={%region_2.5_spmd, %region_5.9_spmd} | conditional | flops 204410160 | bytes 6552408 | solution.py:107
  182.3 0.8 convolution_convert_fusion.1
  183.2 71.1 %all-gather.5.cloned.1.call-done = bf16[1,512,4096]{2,1,0:T(8,128)(2,1)} async-done(((bf16[1,512,256]{2,1,0:T(8,128)(2,1)}), bf16[1,512,4096]{2,1,0:T(8,128)(2,1)}) %all-gather.5.cloned.1.call-update) | async-done | bytes 4194320 | tf_op jit(solution)/shard_map/all_gather | solution.py:109
  254.3 4.8 %convolution_convert_fusion.2 = bf16[256,4096]{1,0:T(8,128)(2,1)} fusion(bf16[256,512]{0,1:T(8,128)(2,1)S(1)} %get-tuple-element.36, bf16[1,512,4096]{2,1,0:T(8,128)(2,1)} %all-gather.5.cloned.1.call-done), kind=kOutput, calls=%fused_computation.48 | convolution fusion | flops 1074790400 | bytes 6553600 | tf_op jit(solution)/shard_map/dot_general | solution.py:111
  259.2 36.3 %reduce-scatter.2.cloned.1.call-done = bf16[256,512]{1,0:T(8,128)(2,1)} async-done(((bf16[256,4096]{1,0:T(8,128)(2,1)}), bf16[256,512]{1,0:T(8,128)(2,1)}) %reduce-scatter.2.cloned.1.call-update) | async-done | bytes 262160 | tf_op jit(solution)/shard_map/reduce_scatter | solution.py:112
  295.4 1.0 add_convert_fusion
  296.5 26.0 %all_to_all.5 = bf16[16,16,512]{2,1,0:T(8,128)(2,1)S(1)} all-to-all(bf16[16,16,512]{2,1,0:T(8,128)(2,1)S(1)} %bitcast.87), channel_id=1, replica_groups=mesh['segment'=4,'seq'=16,'mp'=8] {'seq'}, dimensions={0} | all-to-all | bytes 524288 | tf_op jit(solution)/shard_map/all_to_all | solution.py:36
  322.5 4.8 %collective-permute-start.7 = (bf16[16,16,512]{2,1,0:T(8,128)(2,1)S(1)}, bf16[16,16,512]{2,1,0:T(8,128)(2,1)S(1)}, u32[]{:S(2)}, u32[]{:S(2)}) collective-permute-start(bf16[16,16,512]{2,1,0:T(8,128)(2,1)S(1)} %all_to_all.5), channel_id=1, source_target_pairs={{0,128},{128,256},{256,384},{384,0},{1,129},{129,257},{257,385},{3... | collective-permute-start | bytes 786440 | tf_op jit(solution)/shard_map/ppermute | solution.py:14
  327.3 5.8 %collective-permute-done.7 = bf16[16,16,512]{2,1,0:T(8,128)(2,1)S(1)} collective-permute-done((bf16[16,16,512]{2,1,0:T(8,128)(2,1)S(1)}, bf16[16,16,512]{2,1,0:T(8,128)(2,1)S(1)}, u32[]{:S(2)}, u32[]{:S(2)}) %collective-permute-start.7) | collective-permute-done | bytes 262176 | tf_op jit(solution)/shard_map/ppermute | solution.py:14
  333.1 0.7 copy.40
  (41 shorter events, 5.2 us)
Async XLA Ops:
  6.5 252.6 %copy-start = (f32[1,4096]{1,0:T(1,128)S(1)}, f32[1,4096]{1,0:T(1,128)}, u32[]{:S(2)}) copy-start(f32[1,4096]{1,0:T(1,128)} %param.14) | copy-start | bytes 49156
  6.5 3.2 copy-start.1
  6.5 164.9 %all-gather.3.cloned.1.call-start = ((), (), s32[]{:S(2)}) async-start(), calls=%async_computation.2 | async-start | bytes 13369344 | tf_op jit(solution)/shard_map/all_gather | solution.py:84
  8.9 245.4 %all-gather.5.cloned.1.call-start = ((), (), s32[]{:S(2)}) async-start(), calls=%async_computation.3 | async-start | bytes 4456448 | tf_op jit(solution)/shard_map/all_gather | solution.py:109
  9.7 285.8 %reduce-scatter.2.cloned.1.call-start = ((), (), s32[]{:S(2)}) async-start(), calls=%async_computation.4 | async-start | bytes 2359296 | tf_op jit(solution)/shard_map/reduce_scatter | solution.py:112
  9.7 9.7 %collective-permute-start = (bf16[1,1,256,512]{3,2,1,0:T(8,128)(2,1)S(1)}, bf16[1,1,256,512]{3,2,1,0:T(8,128)(2,1)S(1)}, u32[]{:S(2)}, u32[]{:S(2)}) collective-permute-start(bf16[1,1,256,512]{3,2,1,0:T(8,128)(2,1)S(1)} %copy-done.1), channel_id=1, source_target_pairs={{0,1},{1,2},{2,3},{3,4},{4,5},{5,6},{6,7},{7,0},{8,9},{9,10},{10,1... | collective-permute-start | bytes 786440 | tf_op jit(solution)/shard_map/ppermute | solution.py:59
  13.7 8.2 %collective-permute-start.1 = (bf16[1,1,256,512]{3,2,1,0:T(8,128)(2,1)S(1)}, bf16[1,1,256,512]{3,2,1,0:T(8,128)(2,1)S(1)}, u32[]{:S(2)}, u32[]{:S(2)}) collective-permute-start(bf16[1,1,256,512]{3,2,1,0:T(8,128)(2,1)S(1)} %copy-done.1), channel_id=1, source_target_pairs={{0,7},{1,0},{2,1},{3,2},{4,3},{5,4},{6,5},{7,6},{8,15},{9,8},{10,9... | collective-permute-start | bytes 786440 | tf_op jit(solution)/shard_map/ppermute | solution.py:66
  19.4 9.1 %collective-permute-start.2 = (bf16[1,1,256,512]{3,2,1,0:T(8,128)(2,1)S(1)}, bf16[1,1,256,512]{3,2,1,0:T(8,128)(2,1)S(1)}, u32[]{:S(2)}, u32[]{:S(2)}) collective-permute-start(bf16[1,1,256,512]{3,2,1,0:T(8,128)(2,1)S(1)} %collective-permute-done), channel_id=1, source_target_pairs={{0,1},{1,2},{2,3},{3,4},{4,5},{5,6},{6,7},{7,0},{8,9},{9,10},{10,1... | collective-permute-start | bytes 786440 | tf_op jit(solution)/shard_map/ppermute | solution.py:59
  21.9 8.5 %collective-permute-start.3 = (bf16[1,1,256,512]{3,2,1,0:T(8,128)(2,1)S(1)}, bf16[1,1,256,512]{3,2,1,0:T(8,128)(2,1)S(1)}, u32[]{:S(2)}, u32[]{:S(2)}) collective-permute-start(bf16[1,1,256,512]{3,2,1,0:T(8,128)(2,1)S(1)} %collective-permute-done.1), channel_id=1, source_target_pairs={{0,7},{1,0},{2,1},{3,2},{4,3},{5,4},{6,5},{7,6},{8,15},{9,8},{10,9... | collective-permute-start | bytes 786440 | tf_op jit(solution)/shard_map/ppermute | solution.py:66
  28.4 9.6 %collective-permute-start.4 = (bf16[1,1,256,512]{3,2,1,0:T(8,128)(2,1)S(1)}, bf16[1,1,256,512]{3,2,1,0:T(8,128)(2,1)S(1)}, u32[]{:S(2)}, u32[]{:S(2)}) collective-permute-start(bf16[1,1,256,512]{3,2,1,0:T(8,128)(2,1)S(1)} %collective-permute-done.2), channel_id=1, source_target_pairs={{0,1},{1,2},{2,3},{3,4},{4,5},{5,6},{6,7},{7,0},{8,9},{9,10},{10,1... | collective-permute-start | bytes 786440 | tf_op jit(solution)/shard_map/ppermute | solution.py:59
  30.4 9.6 %collective-permute-start.5 = (bf16[1,1,256,512]{3,2,1,0:T(8,128)(2,1)S(1)}, bf16[1,1,256,512]{3,2,1,0:T(8,128)(2,1)S(1)}, u32[]{:S(2)}, u32[]{:S(2)}) collective-permute-start(bf16[1,1,256,512]{3,2,1,0:T(8,128)(2,1)S(1)} %collective-permute-done.3), channel_id=1, source_target_pairs={{0,7},{1,0},{2,1},{3,2},{4,3},{5,4},{6,5},{7,6},{8,15},{9,8},{10,9... | collective-permute-start | bytes 786440 | tf_op jit(solution)/shard_map/ppermute | solution.py:66
  38.0 10.3 %collective-permute-start.6 = (bf16[1,1,256,512]{3,2,1,0:T(8,128)(2,1)S(1)}, bf16[1,1,256,512]{3,2,1,0:T(8,128)(2,1)S(1)}, u32[]{:S(2)}, u32[]{:S(2)}) collective-permute-start(bf16[1,1,256,512]{3,2,1,0:T(8,128)(2,1)S(1)} %collective-permute-done.4), channel_id=1, source_target_pairs={{0,1},{1,2},{2,3},{3,4},{4,5},{5,6},{6,7},{7,0},{8,9},{9,10},{10,1... | collective-permute-start | bytes 786440 | tf_op jit(solution)/shard_map/ppermute | solution.py:59
  48.3 123.1 %copy-start.3 = (f32[1,4096]{1,0:T(1,128)S(1)}, f32[1,4096]{1,0:T(1,128)}, u32[]{:S(2)}) copy-start(f32[1,4096]{1,0:T(1,128)} %param.12) | copy-start | bytes 49156
  48.4 123.0 %copy-start.4 = (f32[1,4096]{1,0:T(1,128)S(1)}, f32[1,4096]{1,0:T(1,128)}, u32[]{:S(2)}) copy-start(f32[1,4096]{1,0:T(1,128)} %param.13) | copy-start | bytes 49156
  171.4 8.1 %copy-start.2 = (s32[1,16]{1,0:T(1,128)S(1)}, s32[1,16]{1,0:T(1,128)}, u32[]{:S(2)}) copy-start(s32[1,16]{1,0:T(1,128)} %param.15) | copy-start | bytes 196
  322.5 10.6 %collective-permute-start.7 = (bf16[16,16,512]{2,1,0:T(8,128)(2,1)S(1)}, bf16[16,16,512]{2,1,0:T(8,128)(2,1)S(1)}, u32[]{:S(2)}, u32[]{:S(2)}) collective-permute-start(bf16[16,16,512]{2,1,0:T(8,128)(2,1)S(1)} %all_to_all.5), channel_id=1, source_target_pairs={{0,128},{128,256},{256,384},{384,0},{1,129},{129,257},{257,385},{3... | collective-permute-start | bytes 786440 | tf_op jit(solution)/shard_map/ppermute | solution.py:14
Sparse Core Ops, SparseCore 0:
  10.5 160.8 all-gather.2
  174.5 79.7 all-gather.4
  259.2 36.1 reduce-scatter.1
